TPU v7x, 256 devices: a whole 4x4x8 slice. The times are simulated.
256 devices in a mesh: kv: 8 (over y, core), blk: 32 (over x, z).
Axes of the slice: x: 4, y: 4, z: 8, core: 2. Of those that a mesh axis runs over, the one named last changes fastest.
Arguments:
- queries: bfloat16 [256, 8192], P('blk', 'kv'), may hold values from -40 to 40
- draft_token_keys: bfloat16 [256, 1024], P('blk', 'kv'), may hold values from -15 to 15
- draft_token_values: bfloat16 [256, 1024], P('blk', 'kv'), may hold values from -6 to 6
- cached_key_vectors: bfloat16 [4, 4096, 1024], P(None, 'blk', 'kv'), may hold values from -40 to 40
- cached_value_vectors: bfloat16 [4, 4096, 1024], P(None, 'blk', 'kv'), may hold values from -6 to 6
- out_weight: bfloat16 [8192, 8192], P('kv', 'blk'), may hold values from -0.5 to 0.5
- lengths: int32 [4], replicated, may hold values from 256 to 4088, as said below
- parents: int32 [4, 64], replicated, may hold values from 0 to 62, as said below
- accepted_nodes: int32 [4, 8], replicated, may hold values from 0 to 62, as said below
- accepted_count: int32 [4], replicated, may hold values from 1 to 8, as said below
Outputs:
- projected: bfloat16 [256, 8192], P('kv', 'blk')
- new_cache_keys: bfloat16 [4, 4096, 1024], P(None, 'blk', 'kv')
- new_cache_values: bfloat16 [4, 4096, 1024], P(None, 'blk', 'kv')
Inputs may be any that keep to these rules, and one draw needn't show every extreme that they name: `lengths`: some request has exactly 4088, some exactly 256. parents[r, 0] = 0 and parents[r, i] < i for i >= 1. accepted_nodes[r, 0] = 0 and accepted_nodes[r, k] is a child of accepted_nodes[r, k - 1] in request r's tree; only the first accepted_count[r] entries are used. `accepted_count`: some request has exactly 8, some exactly 1.
All inputs are finite; a program needn't handle non-finite values.
Results may differ from a plain program's by a relative error of at most 0.0055.
Values may be sent and summed in bfloat16 or wider, within the bound.
No kernel may reach another device: no remote copies, remote signals or barrier semaphores. Data moves between devices by JAX's collectives and lax.ppermute only.
A program may use at most 64 MiB of HBM per device.

v0:
```python
import math
import jax
import jax.numpy as jnp
from jax import lax
from jax.sharding import PartitionSpec as P

HEAD_SIZE = 128
TREE_TOKENS = 64
ACC = 8
NEG_FLOOR = -1e30


def ancestors(parent_rows):
    node_ids = jnp.arange(TREE_TOKENS, dtype=jnp.int32)
    parent_link = (
        (parent_rows[:, :, None] == node_ids[None, None, :]) & (node_ids[None, :, None] >= 1)
    ).astype(jnp.float32)
    reachable = jnp.eye(TREE_TOKENS, dtype=jnp.float32)[None] + parent_link
    for doubling in range((TREE_TOKENS - 1).bit_length()):
        reachable = jnp.minimum(
            reachable
            + jnp.einsum("rij,rjk->rik", reachable, reachable, precision=lax.Precision.HIGHEST),
            1.0,
        )
    return reachable


def partial_softmax(query_vectors, key_rows, value_rows, usable, score_scale):
    scores = (
        jnp.einsum(
            "rtkgh,rbpkh->brkgtp", query_vectors, key_rows, preferred_element_type=jnp.float32
        )
        * score_scale
    )
    scores = jnp.where(usable, scores, NEG_FLOOR)
    peak_score = jnp.max(scores, axis=-1)
    weights = jnp.where(usable, jnp.exp(scores - peak_score[..., None]), 0.0)
    weight_sum = jnp.sum(weights, axis=-1)
    weighted = jnp.einsum(
        "brkgtp,rbpkh->brtkgh",
        weights.astype(jnp.bfloat16),
        value_rows,
        preferred_element_type=jnp.float32,
    )
    block_count, req_count, kv_count, query_group_width, row_count = peak_score.shape
    weighted = weighted.reshape(
        block_count, req_count * row_count, kv_count * query_group_width * value_rows.shape[-1]
    )
    peak_score = peak_score.transpose(0, 1, 4, 2, 3).reshape(
        block_count, req_count * row_count, kv_count * query_group_width
    )
    weight_sum = weight_sum.transpose(0, 1, 4, 2, 3).reshape(
        block_count, req_count * row_count, kv_count * query_group_width
    )
    return (weighted, peak_score, weight_sum)


def merge_parts(cache_part, draft_part, head_dim):
    cache_out, cache_peak, cache_sum = cache_part
    draft_out, draft_peak, draft_sum = draft_part
    cache_out = cache_out.astype(jnp.float32)
    overall = jnp.maximum(jnp.max(cache_peak, axis=0), draft_peak[0])
    cache_factor = jnp.exp(cache_peak - overall[None])
    draft_factor = jnp.exp(draft_peak[0] - overall)
    denominator = jnp.sum(cache_factor * cache_sum, axis=0) + draft_factor * draft_sum[0]
    block_count, row_count, head_count = cache_peak.shape
    numerator = jnp.sum(
        cache_factor[..., None] * cache_out.reshape(block_count, row_count, head_count, head_dim),
        axis=0,
    )
    numerator = numerator + draft_factor[..., None] * draft_out[0].reshape(
        row_count, head_count, head_dim
    )
    return (
        (numerator / denominator[..., None])
        .reshape(row_count, head_count * head_dim)
        .astype(jnp.bfloat16)
    )


def place_rows(sources, slot_index, written, cache_rows):
    slot_ids = jnp.arange(sources.shape[1], dtype=jnp.int32)
    selector = ((slot_index[:, :, None] == slot_ids[None, None, :]) & written[:, :, None]).astype(
        jnp.bfloat16
    )
    placed = jnp.einsum(
        "rps,rsc->rpc", selector, sources, preferred_element_type=jnp.float32
    ).astype(jnp.bfloat16)
    return jnp.where(written[:, :, None], placed, cache_rows)


def on_device(
    queries,
    draft_token_keys,
    draft_token_values,
    cached_key_vectors,
    cached_value_vectors,
    out_weight,
    lengths,
    parents,
    accepted_nodes,
    accepted_count,
):
    block_count = lax.axis_size("blk")
    my_block = lax.axis_index("blk")
    rows_dev, width_q = queries.shape
    requests = lengths.shape[0]
    cache_width = cached_key_vectors.shape[2]
    kv_local = cache_width // HEAD_SIZE
    query_group_width = width_q // (kv_local * HEAD_SIZE)
    block_len = cached_key_vectors.shape[1]
    score_scale = 1.0 / math.sqrt(HEAD_SIZE)
    leading_row = my_block * rows_dev
    my_request = leading_row // TREE_TOKENS
    node_start = leading_row - my_request * TREE_TOKENS
    local_queries = queries.reshape(1, rows_dev, kv_local, query_group_width, HEAD_SIZE)
    gathered_keys, gathered_values = (
        lax.all_gather(draft_token_keys, "blk", axis=0, tiled=True),
        lax.all_gather(draft_token_values, "blk", axis=0, tiled=True),
    )
    tree_keys = lax.dynamic_slice_in_dim(
        gathered_keys, my_request * TREE_TOKENS, TREE_TOKENS, 0
    ).reshape(1, 1, TREE_TOKENS, kv_local, HEAD_SIZE)
    tree_values = lax.dynamic_slice_in_dim(
        gathered_values, my_request * TREE_TOKENS, TREE_TOKENS, 0
    ).reshape(1, 1, TREE_TOKENS, kv_local, HEAD_SIZE)
    reachable = ancestors(lax.dynamic_slice_in_dim(parents, my_request, 1, 0))
    own_reach = lax.dynamic_slice_in_dim(reachable, node_start, rows_dev, 1)
    draft_usable = (own_reach > 0.5)[None, :, None, None, :, :]
    draft_part = partial_softmax(local_queries, tree_keys, tree_values, draft_usable, score_scale)
    every_query = lax.all_gather(queries, "blk", axis=0, tiled=True)
    all_queries = every_query.reshape(requests, TREE_TOKENS, kv_local, query_group_width, HEAD_SIZE)
    positions = my_block * block_len + jnp.arange(block_len, dtype=jnp.int32)
    usable = (positions[None, :] < lengths[:, None])[None, :, None, None, None, :]
    local_out, local_peak, local_sum = partial_softmax(
        all_queries,
        cached_key_vectors.reshape(requests, 1, block_len, kv_local, HEAD_SIZE),
        cached_value_vectors.reshape(requests, 1, block_len, kv_local, HEAD_SIZE),
        usable,
        score_scale,
    )
    moved_out = lax.all_to_all(
        local_out[0].astype(jnp.bfloat16), "blk", split_axis=0, concat_axis=0, tiled=True
    )
    moved_peak, moved_sum = (
        lax.all_to_all(local_peak[0], "blk", split_axis=0, concat_axis=0, tiled=True),
        lax.all_to_all(local_sum[0], "blk", split_axis=0, concat_axis=0, tiled=True),
    )
    cache_part = (
        moved_out.reshape(block_count, rows_dev, -1),
        moved_peak.reshape(block_count, rows_dev, -1),
        moved_sum.reshape(block_count, rows_dev, -1),
    )
    attention = merge_parts(cache_part, draft_part, HEAD_SIZE)
    every_row = lax.all_gather(attention, "blk", axis=0, tiled=True)
    projected = lax.psum_scatter(
        jnp.dot(every_row, out_weight, preferred_element_type=jnp.float32),
        "kv",
        scatter_dimension=0,
        tiled=True,
    ).astype(jnp.bfloat16)
    positions_here = my_block * block_len + jnp.arange(block_len, dtype=jnp.int32)
    offset = positions_here[None, :] - lengths[:, None]
    written = (offset >= 0) & (offset < accepted_count[:, None])
    slot_match = offset[:, :, None] == jnp.arange(ACC, dtype=jnp.int32)[None, None, :]
    node_ids = jnp.sum(jnp.where(slot_match, accepted_nodes[:, None, :], 0), axis=-1)
    new_cache_keys = place_rows(
        gathered_keys.reshape(requests, TREE_TOKENS, cache_width),
        node_ids,
        written,
        cached_key_vectors,
    )
    new_cache_values = place_rows(
        gathered_values.reshape(requests, TREE_TOKENS, cache_width),
        node_ids,
        written,
        cached_value_vectors,
    )
    return (projected, new_cache_keys, new_cache_values)


def solution(mesh):
    return jax.shard_map(
        on_device,
        mesh=mesh,
        in_specs=(
            P("blk", "kv"),
            P("blk", "kv"),
            P("blk", "kv"),
            P(None, "blk", "kv"),
            P(None, "blk", "kv"),
            P("kv", "blk"),
            P(),
            P(),
            P(),
            P(),
        ),
        out_specs=(P("kv", "blk"), P(None, "blk", "kv"), P(None, "blk", "kv")),
        check_vma=False,
    )
```

profile of v0, /device:TPU:4, one launch (start us, length us, event | category | flops | bytes accessed | tf_op | source)
XLA Modules:
  0.0 283.2 jit_solution(6626827668490179836)
XLA Ops:
  7.2 0.0 copy-start
  7.2 52.1 %all_gather.12 = bf16[256,1024]{1,0:T(8,128)(2,1)S(1)} all-gather(bf16[8,1024]{1,0:T(8,128)(2,1)} %param.10), channel_id=1, replica_groups=mesh['kv'=8,'blk'=32] {'blk'}, dimensions={0}, use_global_device_ids=true | all-gather | bytes 540672 | tf_op jit(solution)/shard_map/all_gather | solution.py:131
  59.3 0.0 copy-start.6
  59.3 0.0 copy-start.7
  59.3 0.0 copy-start.8
  59.4 0.1 copy.86
  59.5 0.5 copy-done.6
  60.0 0.0 copy-done.7
  60.0 0.1 compare_and_fusion
  60.1 0.2 copy-done.8
  60.3 0.5 fusion.53
  60.8 0.1 all_to_all.16
  60.9 0.7 copy.63
  61.7 7.0 %all-to-all-start = ((f32[32,8,8]{1,2,0:T(8,128)}), f32[32,8,8]{1,2,0:T(8,128)S(1)}, u32[]{:S(2)}, u32[]{:S(2)}) async-start(f32[32,8,8]{1,2,0:T(8,128)} %copy.63), calls=%async_computation | async-start | bytes 262144 | tf_op jit(solution)/shard_map/all_to_all | solution.py:146
  68.7 0.7 fusion.51
  69.4 0.2 fusion.35
  69.6 0.2 fusion.14
  69.7 0.2 fusion.6
  69.9 0.2 fusion.7
  70.1 0.2 fusion.8
  70.3 0.2 fusion.9
  70.4 0.2 fusion.55
  70.6 0.0 copy-start.1
  70.6 0.6 fusion.18
  71.3 0.2 copy-done.1
  71.5 0.5 fusion.3
  72.0 0.1 all_to_all.19
  72.1 0.7 copy.73
  72.9 0.3 copy.69
  73.2 1.0 convert_element_type.101
  74.2 0.0 copy-start.3
  74.2 2.8 all-to-all-done
  77.0 7.1 %all-to-all-start.2 = ((f32[32,8,8]{1,2,0:T(8,128)}), f32[32,8,8]{1,2,0:T(8,128)S(1)}, u32[]{:S(2)}, u32[]{:S(2)}) async-start(f32[32,8,8]{1,2,0:T(8,128)} %copy.73), calls=%async_computation.2 | async-start | bytes 262144 | tf_op jit(solution)/shard_map/all_to_all | solution.py:147
  84.2 0.0 copy-done.3
  84.2 49.3 %all_gather.13 = bf16[256,128]{1,0:T(8,128)(2,1)S(1)} all-gather(bf16[8,128]{1,0:T(8,128)(2,1)S(1)} %copy-done.3), channel_id=1, replica_groups=mesh['kv'=8,'blk'=32] {'blk'}, dimensions={0}, use_global_device_ids=true | all-gather | bytes 67584 | tf_op jit(solution)/shard_map/all_gather | solution.py:118
  133.4 0.0 copy-start.2
  133.4 0.0 all-to-all-done.2
  133.5 7.9 %all-to-all-start.1 = ((bf16[32,8,1024]{2,1,0:T(8,128)(2,1)}), bf16[32,8,1024]{2,1,0:T(8,128)(2,1)S(1)}, u32[]{:S(2)}, u32[]{:S(2)}) async-start(bf16[32,8,1024]{2,1,0:T(8,128)(2,1)} %convert_element_type.101), calls=%async_computation.1 | async-start | bytes 1048576 | tf_op jit(solution)/shard_map/all_to_all | solution.py:142
  141.4 0.0 reduce-scatter.2.cloned.1.call-start
  141.4 0.0 copy-done.2
  141.4 0.2 fusion.54
  141.6 0.2 fusion.37
  141.8 0.1 copy.75
  141.9 0.0 copy-start.4
  141.9 0.1 copy.68
  141.9 0.6 copy-done.4
  142.6 49.7 %all_gather.14 = bf16[256,128]{1,0:T(8,128)(2,1)S(1)} all-gather(bf16[8,128]{1,0:T(8,128)(2,1)S(1)} %copy-done.4), channel_id=1, replica_groups=mesh['kv'=8,'blk'=32] {'blk'}, dimensions={0}, use_global_device_ids=true | all-gather | bytes 67584 | tf_op jit(solution)/shard_map/all_gather | solution.py:119
  192.2 0.1 broadcast_subtract_fusion
  192.4 0.0 all-to-all-done.1
  192.4 0.3 fusion.17
  192.8 0.1 fusion.15
  192.9 47.4 %all_gather.15 = bf16[256,1024]{1,0:T(8,128)(2,1)S(1)} all-gather(bf16[8,1024]{1,0:T(8,128)(2,1)S(1)} %fusion.15), channel_id=1, replica_groups=mesh['kv'=8,'blk'=32] {'blk'}, dimensions={0}, use_global_device_ids=true | all-gather | bytes 540672 | tf_op jit(solution)/shard_map/all_gather | solution.py:155
  240.3 0.0 copy-done
  240.3 1.0 fusion.56
  241.3 0.0 copy-start.5
  241.3 0.0 reduce-scatter.2.cloned.1.call-update
  241.3 0.7 copy-done.5
  242.0 0.1 select_reduce_fusion
  242.0 0.9 fusion.4
  243.0 0.9 fusion.5
  243.9 31.1 %reduce-scatter.2.cloned.1.call-done = f32[32,256]{1,0:T(8,128)} async-done(((f32[256,256]{1,0:T(8,128)}), f32[32,256]{1,0:T(8,128)}) %reduce-scatter.2.cloned.1.call-update) | async-done | bytes 32784 | tf_op jit(solution)/shard_map/reduce_scatter | solution.py:156
  274.9 1.4 convert_element_type.105
  (9 shorter events, 0.1 us)
Async XLA Ops:
  7.2 233.1 %copy-start = (bf16[1024,256]{1,0:T(8,128)(2,1)S(1)}, bf16[1024,256]{1,0:T(8,128)(2,1)}, u32[]{:S(2)}) copy-start(bf16[1024,256]{1,0:T(8,128)(2,1)} %param.15) | copy-start | bytes 1572868
  59.3 0.7 copy-start.6
  59.3 0.7 copy-start.7
  59.3 0.9 copy-start.8
  61.7 15.4 %all-to-all-start = ((f32[32,8,8]{1,2,0:T(8,128)}), f32[32,8,8]{1,2,0:T(8,128)S(1)}, u32[]{:S(2)}, u32[]{:S(2)}) async-start(f32[32,8,8]{1,2,0:T(8,128)} %copy.63), calls=%async_computation | async-start | bytes 262144 | tf_op jit(solution)/shard_map/all_to_all | solution.py:146
  70.6 0.9 copy-start.1
  74.2 9.9 %copy-start.3 = (bf16[8,128]{1,0:T(8,128)(2,1)S(1)}, bf16[8,128]{1,0:T(8,128)(2,1)}, u32[]{:S(2)}) copy-start(bf16[8,128]{1,0:T(8,128)(2,1)} %param.11) | copy-start | bytes 6148
  77.0 56.4 %all-to-all-start.2 = ((f32[32,8,8]{1,2,0:T(8,128)}), f32[32,8,8]{1,2,0:T(8,128)S(1)}, u32[]{:S(2)}, u32[]{:S(2)}) async-start(f32[32,8,8]{1,2,0:T(8,128)} %copy.73), calls=%async_computation.2 | async-start | bytes 262144 | tf_op jit(solution)/shard_map/all_to_all | solution.py:147
  133.4 8.0 %copy-start.2 = (bf16[8,1024]{1,0:T(8,128)(2,1)S(1)}, bf16[8,1024]{1,0:T(8,128)(2,1)}, u32[]{:S(2)}) copy-start(bf16[8,1024]{1,0:T(8,128)(2,1)} %param.10) | copy-start | bytes 49156
  133.5 59.0 %all-to-all-start.1 = ((bf16[32,8,1024]{2,1,0:T(8,128)(2,1)}), bf16[32,8,1024]{2,1,0:T(8,128)(2,1)S(1)}, u32[]{:S(2)}, u32[]{:S(2)}) async-start(bf16[32,8,1024]{2,1,0:T(8,128)(2,1)} %convert_element_type.101), calls=%async_computation.1 | async-start | bytes 1048576 | tf_op jit(solution)/shard_map/all_to_all | solution.py:142
  141.4 133.6 %reduce-scatter.2.cloned.1.call-start = ((), (), s32[]{:S(2)}) async-start(), calls=%async_computation.4 | async-start | bytes 294912 | tf_op jit(solution)/shard_map/reduce_scatter | solution.py:156
  141.9 0.7 copy-start.4
  241.3 0.7 copy-start.5
Sparse Core Ops, SparseCore 0:
  241.4 33.4 reduce-scatter.1
where the time goes:
time: 284 us; the launch traced here: 283 us
  blocking collectives  198 us (70%)
  waiting for transfers between devices  33.9 us (12%)
  starting transfers between devices  22 us (8%)
  between operations  14.3 us (5%)
  local copies, waits for them, and re-layouts  6.25 us (2%)
  matrix products  5.14 us (2%)
  other arithmetic  3.09 us (1%)
    all_gather x1, blocking collectives, on_device(): every_query = lax.all_gather(queries, 'blk', axis=0, tiled=True)  52.1 us
    all_gather x1, blocking collectives, on_device(): lax.all_gather(draft_token_values, 'blk', axis=0, tiled=True)  49.7 us
    all_gather x1, blocking collectives, on_device(): lax.all_gather(draft_token_keys, 'blk', axis=0, tiled=True)  49.3 us
    all_gather x1, blocking collectives, on_device(): every_row = lax.all_gather(attention, 'blk', axis=0, tiled=True)  47.4 us
    reduce_scatter x1, waiting for transfers between devices, on_device(): lax.psum_scatter(jnp.dot(every_row, out_weight, preferred_element_type=jn...  31.1 us
    all_to_all x1, starting transfers between devices, on_device(): lax.all_to_all(local_out[0].astype(jnp.bfloat16), 'blk', split_axis=0, co...  7.89 us
    all_to_all x1, starting transfers between devices, on_device(): lax.all_to_all(local_sum[0], 'blk', split_axis=0, concat_axis=0, tiled=True)  7.09 us
    all_to_all x1, starting transfers between devices, on_device(): lax.all_to_all(local_peak[0], 'blk', split_axis=0, concat_axis=0, tiled=T...  6.95 us
  transfers between devices with their start and end apart: 4, of which 2 were waited for; matrix products, arithmetic and copies ran while one was open for 3% of the time, Pallas kernels for 0%

commit v1 on v0

--- a/solution.py
+++ b/solution.py
@@ -116,7 +116,10 @@
     local_queries = queries.reshape(1, rows_dev, kv_local, query_group_width, HEAD_SIZE)
     gathered_keys, gathered_values = (
         lax.all_gather(draft_token_keys, "blk", axis=0, tiled=True),
-        lax.all_gather(draft_token_values, "blk", axis=0, tiled=True),
+        jnp.concatenate(
+            lax.all_to_all(jnp.stack([draft_token_values] * lax.axis_size("blk")), "blk", 0, 0),
+            axis=0,
+        ),
     )
     tree_keys = lax.dynamic_slice_in_dim(
         gathered_keys, my_request * TREE_TOKENS, TREE_TOKENS, 0

time: 284 us -> 258 us (0.908)
  blocking collectives: 198 us -> 149 us
  waiting for transfers between devices: 33.9 us -> 50 us
  starting transfers between devices: 22 us -> 29.5 us
    all_gather x1 -> x0, blocking collectives: 49.7 us -> none  [on_device(): lax.all_gather(draft_token_values, 'blk', axis=0, tiled=True)]
    all_to_all x1, waiting for transfers between devices: 0.01 us -> 10.1 us  [on_device(): lax.all_to_all(local_out[0].astype(jnp.bfloat16), 'blk', split_axis=0, co...]
    all_to_all x0 -> x1, waiting for transfers between devices: none -> 7.62 us  [on_device(): lax.all_to_all(jnp.stack([draft_token_values] * lax.axis_size('blk')), 'b...]
    all_to_all x0 -> x1, starting transfers between devices: none -> 7.5 us  [on_device(): lax.all_to_all(jnp.stack([draft_token_values] * lax.axis_size('blk')), 'b...]
  transfers between devices with their start and end apart: 4 -> 5, of which waited for: 2 -> 4; matrix products, arithmetic and copies ran while one was open for 3% -> 3% of each run, Pallas kernels for 0% -> 0%
where the time goes in v1:
time: 258 us; the launch traced here: 257 us
  blocking collectives  149 us (58%)
  waiting for transfers between devices  50 us (19%)
  starting transfers between devices  29.5 us (11%)
  between operations  14.3 us (6%)
  local copies, waits for them, and re-layouts  6.28 us (2%)
  matrix products  5.14 us (2%)
  other arithmetic  3.08 us (1%)
    all_gather x1, blocking collectives, on_device(): every_query = lax.all_gather(queries, 'blk', axis=0, tiled=True)  52.1 us
    all_gather x1, blocking collectives, on_device(): lax.all_gather(draft_token_keys, 'blk', axis=0, tiled=True)  49.3 us
    all_gather x1, blocking collectives, on_device(): every_row = lax.all_gather(attention, 'blk', axis=0, tiled=True)  47.6 us
    reduce_scatter x1, waiting for transfers between devices, on_device(): lax.psum_scatter(jnp.dot(every_row, out_weight, preferred_element_type=jn...  29.5 us
    all_to_all x1, waiting for transfers between devices, on_device(): lax.all_to_all(local_out[0].astype(jnp.bfloat16), 'blk', split_axis=0, co...  10.1 us
    all_to_all x1, starting transfers between devices, on_device(): lax.all_to_all(local_out[0].astype(jnp.bfloat16), 'blk', split_axis=0, co...  7.89 us
    all_to_all x1, waiting for transfers between devices, on_device(): lax.all_to_all(jnp.stack([draft_token_values] * lax.axis_size('blk')), 'b...  7.62 us
    all_to_all x1, starting transfers between devices, on_device(): lax.all_to_all(jnp.stack([draft_token_values] * lax.axis_size('blk')), 'b...  7.5 us
  transfers between devices with their start and end apart: 5, of which 4 were waited for; matrix products, arithmetic and copies ran while one was open for 3% of the time, Pallas kernels for 0%

profile of v1, /device:TPU:4, one launch (start us, length us, event | category | flops | bytes accessed | tf_op | source)
XLA Modules:
  0.0 257.3 jit_solution(16718428132875171701)
XLA Ops:
  7.2 0.0 copy-start
  7.2 52.1 %all_gather.9 = bf16[256,1024]{1,0:T(8,128)(2,1)S(1)} all-gather(bf16[8,1024]{1,0:T(8,128)(2,1)} %param.10), channel_id=1, replica_groups=mesh['kv'=8,'blk'=32] {'blk'}, dimensions={0}, use_global_device_ids=true | all-gather | bytes 540672 | tf_op jit(solution)/shard_map/all_gather | solution.py:134
  59.3 0.0 copy-start.6
  59.3 0.0 copy-start.7
  59.3 0.0 copy-start.8
  59.4 0.1 copy.86
  59.5 0.5 copy-done.6
  60.0 0.0 copy-done.7
  60.0 0.1 compare_and_fusion
  60.1 0.2 copy-done.8
  60.3 0.5 fusion.53
  60.8 0.1 all_to_all.19
  60.9 0.7 copy.63
  61.7 7.0 %all-to-all-start = ((f32[32,8,8]{1,2,0:T(8,128)}), f32[32,8,8]{1,2,0:T(8,128)S(1)}, u32[]{:S(2)}, u32[]{:S(2)}) async-start(f32[32,8,8]{1,2,0:T(8,128)} %copy.63), calls=%async_computation | async-start | bytes 262144 | tf_op jit(solution)/shard_map/all_to_all | solution.py:149
  68.7 0.7 fusion.51
  69.4 0.2 fusion.35
  69.6 0.2 fusion.14
  69.7 0.2 fusion.6
  69.9 0.2 fusion.7
  70.1 0.2 fusion.8
  70.3 0.2 fusion.9
  70.4 0.2 fusion.55
  70.6 0.0 copy-start.1
  70.6 0.6 fusion.18
  71.3 0.2 copy-done.1
  71.5 0.5 fusion.3
  72.0 0.1 all_to_all.23
  72.1 0.7 copy.73
  72.9 0.3 copy.69
  73.2 1.0 convert_element_type.101
  74.2 0.0 copy-start.3
  74.2 2.8 %all-to-all-done = f32[32,8,8]{1,2,0:T(8,128)S(1)} async-done(((f32[32,8,8]{1,2,0:T(8,128)}), f32[32,8,8]{1,2,0:T(8,128)S(1)}, u32[]{:S(2)}, u32[]{:S(2)}) %all-to-all-start) | async-done | bytes 8224 | tf_op jit(solution)/shard_map/all_to_all | solution.py:149
  77.0 7.1 %all-to-all-start.3 = ((f32[32,8,8]{1,2,0:T(8,128)}), f32[32,8,8]{1,2,0:T(8,128)S(1)}, u32[]{:S(2)}, u32[]{:S(2)}) async-start(f32[32,8,8]{1,2,0:T(8,128)} %copy.73), calls=%async_computation.3 | async-start | bytes 262144 | tf_op jit(solution)/shard_map/all_to_all | solution.py:150
  84.2 0.0 copy-done.3
  84.2 49.3 %all_gather.10 = bf16[256,128]{1,0:T(8,128)(2,1)S(1)} all-gather(bf16[8,128]{1,0:T(8,128)(2,1)S(1)} %copy-done.3), channel_id=1, replica_groups=mesh['kv'=8,'blk'=32] {'blk'}, dimensions={0}, use_global_device_ids=true | all-gather | bytes 67584 | tf_op jit(solution)/shard_map/all_gather | solution.py:118
  133.4 0.0 copy-start.2
  133.4 0.0 all-to-all-done.3
  133.5 7.9 %all-to-all-start.1 = ((bf16[32,8,1024]{2,1,0:T(8,128)(2,1)}), bf16[32,8,1024]{2,1,0:T(8,128)(2,1)S(1)}, u32[]{:S(2)}, u32[]{:S(2)}) async-start(bf16[32,8,1024]{2,1,0:T(8,128)(2,1)} %convert_element_type.101), calls=%async_computation.1 | async-start | bytes 1048576 | tf_op jit(solution)/shard_map/all_to_all | solution.py:145
  141.4 0.0 copy-done.2
  141.4 0.2 fusion.54
  141.6 0.2 fusion.37
  141.7 0.1 copy.75
  141.8 0.1 copy.68
  141.9 0.1 broadcast_subtract_fusion
  142.1 0.0 copy-start.4
  142.1 10.1 %all-to-all-done.1 = bf16[32,8,1024]{2,1,0:T(8,128)(2,1)S(1)} async-done(((bf16[32,8,1024]{2,1,0:T(8,128)(2,1)}), bf16[32,8,1024]{2,1,0:T(8,128)(2,1)S(1)}, u32[]{:S(2)}, u32[]{:S(2)}) %all-to-all-start.1) | async-done | bytes 524320 | tf_op jit(solution)/shard_map/all_to_all | solution.py:145
  152.2 0.0 copy-done.4
  152.2 0.6 stack.2
  152.8 7.5 %all-to-all-start.2 = ((bf16[32,8,128]{2,1,0:T(8,128)(2,1)}), bf16[32,8,128]{2,1,0:T(8,128)(2,1)S(1)}, u32[]{:S(2)}, u32[]{:S(2)}) async-start(bf16[32,8,128]{2,1,0:T(8,128)(2,1)} %stack.2), calls=%async_computation.2 | async-start | bytes 131072 | tf_op jit(solution)/shard_map/all_to_all | solution.py:120
  160.3 0.0 reduce-scatter.2.cloned.1.call-start
  160.4 0.3 fusion.17
  160.7 7.6 %all-to-all-done.2 = bf16[32,8,128]{2,1,0:T(8,128)(2,1)S(1)} async-done(((bf16[32,8,128]{2,1,0:T(8,128)(2,1)}), bf16[32,8,128]{2,1,0:T(8,128)(2,1)S(1)}, u32[]{:S(2)}, u32[]{:S(2)}) %all-to-all-start.2) | async-done | bytes 65568 | tf_op jit(solution)/shard_map/all_to_all | solution.py:120
  168.3 0.1 fusion.15
  168.5 47.6 %all_gather.11 = bf16[256,1024]{1,0:T(8,128)(2,1)S(1)} all-gather(bf16[8,1024]{1,0:T(8,128)(2,1)S(1)} %fusion.15), channel_id=1, replica_groups=mesh['kv'=8,'blk'=32] {'blk'}, dimensions={0}, use_global_device_ids=true | all-gather | bytes 540672 | tf_op jit(solution)/shard_map/all_gather | solution.py:158
  216.0 0.0 copy-done
  216.0 1.0 fusion.56
  217.0 0.0 copy-start.5
  217.0 0.0 reduce-scatter.2.cloned.1.call-update
  217.0 0.7 copy-done.5
  217.7 0.1 select_reduce_fusion
  217.8 0.9 fusion.4
  218.7 0.9 fusion.5
  219.6 29.5 %reduce-scatter.2.cloned.1.call-done = f32[32,256]{1,0:T(8,128)} async-done(((f32[256,256]{1,0:T(8,128)}), f32[32,256]{1,0:T(8,128)}) %reduce-scatter.2.cloned.1.call-update) | async-done | bytes 32784 | tf_op jit(solution)/shard_map/reduce_scatter | solution.py:159
  249.1 1.4 convert_element_type.105
  (9 shorter events, 0.1 us)
Async XLA Ops:
  7.2 208.9 %copy-start = (bf16[1024,256]{1,0:T(8,128)(2,1)S(1)}, bf16[1024,256]{1,0:T(8,128)(2,1)}, u32[]{:S(2)}) copy-start(bf16[1024,256]{1,0:T(8,128)(2,1)} %param.15) | copy-start | bytes 1572868
  59.3 0.7 copy-start.6
  59.3 0.7 copy-start.7
  59.3 0.9 copy-start.8
  61.7 15.4 %all-to-all-start = ((f32[32,8,8]{1,2,0:T(8,128)}), f32[32,8,8]{1,2,0:T(8,128)S(1)}, u32[]{:S(2)}, u32[]{:S(2)}) async-start(f32[32,8,8]{1,2,0:T(8,128)} %copy.63), calls=%async_computation | async-start | bytes 262144 | tf_op jit(solution)/shard_map/all_to_all | solution.py:149
  70.6 0.9 copy-start.1
  74.2 9.9 %copy-start.3 = (bf16[8,128]{1,0:T(8,128)(2,1)S(1)}, bf16[8,128]{1,0:T(8,128)(2,1)}, u32[]{:S(2)}) copy-start(bf16[8,128]{1,0:T(8,128)(2,1)} %param.11) | copy-start | bytes 6148
  77.0 56.4 %all-to-all-start.3 = ((f32[32,8,8]{1,2,0:T(8,128)}), f32[32,8,8]{1,2,0:T(8,128)S(1)}, u32[]{:S(2)}, u32[]{:S(2)}) async-start(f32[32,8,8]{1,2,0:T(8,128)} %copy.73), calls=%async_computation.3 | async-start | bytes 262144 | tf_op jit(solution)/shard_map/all_to_all | solution.py:150
  133.4 7.9 %copy-start.2 = (bf16[8,1024]{1,0:T(8,128)(2,1)S(1)}, bf16[8,1024]{1,0:T(8,128)(2,1)}, u32[]{:S(2)}) copy-start(bf16[8,1024]{1,0:T(8,128)(2,1)} %param.10) | copy-start | bytes 49156
  133.5 18.7 %all-to-all-start.1 = ((bf16[32,8,1024]{2,1,0:T(8,128)(2,1)}), bf16[32,8,1024]{2,1,0:T(8,128)(2,1)S(1)}, u32[]{:S(2)}, u32[]{:S(2)}) async-start(bf16[32,8,1024]{2,1,0:T(8,128)(2,1)} %convert_element_type.101), calls=%async_computation.1 | async-start | bytes 1048576 | tf_op jit(solution)/shard_map/all_to_all | solution.py:145
  142.1 10.1 %copy-start.4 = (bf16[8,128]{1,0:T(8,128)(2,1)S(1)}, bf16[8,128]{1,0:T(8,128)(2,1)}, u32[]{:S(2)}) copy-start(bf16[8,128]{1,0:T(8,128)(2,1)} %param.12) | copy-start | bytes 6148
  152.8 15.5 %all-to-all-start.2 = ((bf16[32,8,128]{2,1,0:T(8,128)(2,1)}), bf16[32,8,128]{2,1,0:T(8,128)(2,1)S(1)}, u32[]{:S(2)}, u32[]{:S(2)}) async-start(bf16[32,8,128]{2,1,0:T(8,128)(2,1)} %stack.2), calls=%async_computation.2 | async-start | bytes 131072 | tf_op jit(solution)/shard_map/all_to_all | solution.py:120
  160.3 88.7 %reduce-scatter.2.cloned.1.call-start = ((), (), s32[]{:S(2)}) async-start(), calls=%async_computation.5 | async-start | bytes 294912 | tf_op jit(solution)/shard_map/reduce_scatter | solution.py:159
  217.0 0.7 copy-start.5
Sparse Core Ops, SparseCore 0:
  217.2 31.8 reduce-scatter.1
